TPU v7x, 256 devices: a whole 4x4x8 slice. The times are simulated.
256 devices in a mesh: row: 8 (over z_lo, y), col: 32 (over z_hi, x, core).
Axes of the slice: x: 4, y: 4, z: 8 (z_hi: 4, z_lo: 2; z = z_hi * 2 + z_lo), core: 2. Of those that a mesh axis runs over, the one named last changes fastest.
Arguments:
- strip: float32 [12, 2048, 2, 1024], P(None, 'col', None, 'row'), may hold values from -6 to 6
- lower: float32 [12, 2048, 2, 1024], P(None, 'col', None, 'row'), may hold values from -1.6 to 1.6, as said below
Outputs:
- reduced: float32 [12, 2048, 2, 1024], P(None, 'col', None, 'row')
Inputs may be any that keep to these rules, and one draw needn't show every extreme that they name: `lower`: in the first 2048 rows the diagonal lies between 0.8 and 1.6 and entries above it are zero.
All inputs are finite; a program needn't handle non-finite values.
Results may differ from a plain program's by a relative error of at most 0.00013.
Values sent between devices are 32-bit elements; how exact they have to be, the bound alone decides.
No kernel may reach another device: no remote copies, remote signals or barrier semaphores. Data moves between devices by JAX's collectives and lax.ppermute only.
A program may use at most 64 MiB of HBM per device.

v0:
```python
import jax
import jax.numpy as jnp
from jax import lax
from jax.sharding import PartitionSpec as P

highest = lax.Precision.HIGHEST


def spread(array, axis, root):
    mine = lax.axis_index(axis) == root
    return lax.psum(jnp.where(mine, array, jnp.zeros_like(array)), axis)


def times_rows(coeff, right_side):
    return jnp.dot(coeff, right_side, precision=highest, preferred_element_type=jnp.float32)


def times_rows_turned(coeff, right_turned):
    return lax.dot_general(
        coeff,
        right_turned,
        (((1,), (1,)), ((), ())),
        precision=highest,
        preferred_element_type=jnp.float32,
    )


def local(strip, lower):
    rounds = strip.shape[0]
    strip_width = strip.shape[1]
    row_run = strip.shape[3]
    row_count = lax.axis_size("row")
    block_size = row_run * row_count
    cols_here = rounds * strip_width
    trail_count = cols_here - strip_width
    local_strip = strip.reshape(cols_here, 2, row_run)
    left_part = local_strip[:, 0, :]
    right_part = local_strip[:, 1, :]
    gathered = lax.all_gather(lower[0], "col", axis=0, tiled=True)
    first_cols = gathered[:block_size, 0, :]
    cross_cols = gathered[block_size:, 0, :]
    second_cols = gathered[block_size:, 1, :]
    inverse_all = lax.all_gather(second_cols, "row", axis=1, tiled=True)
    mixed_cols = jnp.dot(
        inverse_all, cross_cols, precision=highest, preferred_element_type=jnp.float32
    )
    upper_half = lax.psum_scatter(
        times_rows_turned(first_cols, left_part), "row", scatter_dimension=0, tiled=True
    )
    carried = lax.psum_scatter(
        times_rows(cross_cols, upper_half), "row", scatter_dimension=0, tiled=True
    )
    remainder = right_part.T - carried
    lower_half = lax.psum_scatter(
        times_rows(second_cols, remainder), "row", scatter_dimension=0, tiled=True
    )
    solved = jnp.stack([upper_half.T, lower_half.T], axis=1)
    lead_rows = solved[:strip_width].reshape(strip_width, 2 * row_run)
    tail_rows = solved[strip_width:].reshape(trail_count, 2 * row_run)
    col_position = lax.axis_index("col")
    offset = col_position * strip_width
    part_block = offset // block_size
    inside = offset % block_size
    root_row = inside // row_run
    shift_in = inside % row_run
    zero_index = jnp.zeros((), jnp.int32)
    mirror_piece = lax.dynamic_slice(
        gathered, (zero_index, part_block, shift_in), (2 * block_size, 1, strip_width)
    )
    mirror_piece = mirror_piece.reshape(2 * block_size, strip_width)
    mirrored = spread(mirror_piece, "row", root_row)
    first_flag = (part_block == 0).astype(jnp.float32)
    second_flag = 1.0 - first_flag
    row_position = lax.axis_index("row")
    first_rows = lax.dynamic_slice_in_dim(mirrored, row_position * row_run, row_run, 0)
    partial_mix = jnp.dot(
        mixed_cols, first_rows, precision=highest, preferred_element_type=jnp.float32
    )
    chained = lax.psum(partial_mix, "row")
    coeff_whole = jnp.concatenate(
        [
            first_flag * mirrored[:block_size],
            second_flag * mirrored[block_size:] - first_flag * chained,
        ],
        axis=0,
    )
    solved_lead = lax.psum_scatter(
        times_rows(coeff_whole, lead_rows), "col", scatter_dimension=0, tiled=True
    )
    everything = lax.all_gather(solved_lead, "col", axis=0, tiled=True)
    left_rows = lower[1:].reshape(trail_count, 2 * row_run)
    grouped = everything.reshape(2, row_count, row_run, 2 * row_run).transpose(1, 0, 2, 3)
    swapped = lax.all_to_all(grouped, "row", split_axis=0, concat_axis=0, tiled=True)
    turned_block = swapped.reshape(row_count, 2, row_run, 2, row_run).transpose(0, 3, 4, 1, 2)
    turned_block = turned_block.reshape(row_count * 2 * row_run, 2 * row_run)
    summed = lax.psum_scatter(
        times_rows_turned(turned_block, left_rows), "row", scatter_dimension=0, tiled=True
    )
    update = summed.T
    reduced = jnp.concatenate([solved_lead, tail_rows - update], axis=0)
    return reduced.reshape(rounds, strip_width, 2, row_run)


def solution(mesh):
    in_specs = (P(None, "col", None, "row"), P(None, "col", None, "row"))
    out_specs = P(None, "col", None, "row")
    return jax.shard_map(local, mesh=mesh, in_specs=in_specs, out_specs=out_specs, check_vma=False)
```

profile of v0, /device:TPU:1, one launch (start us, length us, event | category | flops | bytes accessed | tf_op | source)
XLA Modules:
  0.0 760.2 jit_solution(14494232658817926773)
XLA Ops:
  6.5 1.5 slice_bitcast_fusion.3
  9.3 59.5 %all-gather.8.cloned.1.call-done = f32[1,2048,2,128]{3,2,0,1:T(2,128)} async-done(((f32[1,64,2,128]{3,2,0,1:T(2,128)}), f32[1,2048,2,128]{3,2,0,1:T(2,128)}) %all-gather.8.cloned.1.call-update) | async-done | bytes 2097168 | tf_op jit(solution)/shard_map/all_gather | solution.py:39
  68.8 4.1 fusion.20
  73.0 4.3 fusion.14
  78.2 3.5 constant_dynamic-slice_fusion
  83.3 35.7 %reduce-scatter.6.cloned.1.call-done = f32[128,768]{1,0:T(8,128)} async-done(((f32[1024,768]{1,0:T(8,128)}), f32[128,768]{1,0:T(8,128)}) %reduce-scatter.6.cloned.1.call-update) | async-done | bytes 393232 | tf_op jit(solution)/shard_map/reduce_scatter | solution.py:47
  118.9 5.3 convolution_bitcast_fusion.1
  124.3 97.1 %all-gather.10.cloned.1.call-done = f32[1024,1,1024]{2,1,0:T(1,128)} async-done(((f32[1024,1,128]{2,1,0:T(1,128)}), f32[1024,1,1024]{2,1,0:T(1,128)}) %all-gather.10.cloned.1.call-update) | async-done | bytes 4194320 | tf_op jit(solution)/shard_map/all_gather | solution.py:43
  221.5 5.7 fusion
  227.2 74.9 %all-reduce.3.cloned.1.call-done = f32[2048,64]{0,1:T(8,128)} async-done(((f32[2048,64]{0,1:T(8,128)}), f32[2048,64]{0,1:T(8,128)}) %all-reduce.3.cloned.1.call-update) | async-done | bytes 524304 | tf_op jit(solution)/shard_map/psum | solution.py:11
  302.1 2.2 fusion.16
  304.5 49.9 %reduce-scatter.8.cloned.1.call-done = f32[128,768]{0,1:T(8,128)} async-done(((f32[1024,768]{0,1:T(8,128)}), f32[128,768]{0,1:T(8,128)}) %reduce-scatter.8.cloned.1.call-update) | async-done | bytes 393232 | tf_op jit(solution)/shard_map/reduce_scatter | solution.py:50
  354.4 5.3 convolution_bitcast_fusion
  359.8 74.5 %all-reduce.5.cloned.1.call-done = f32[1024,64]{0,1:T(8,128)} async-done(((f32[1024,64]{0,1:T(8,128)}), f32[1024,64]{0,1:T(8,128)}) %all-reduce.5.cloned.1.call-update) | async-done | bytes 262160 | tf_op jit(solution)/shard_map/psum | solution.py:79
  435.3 50.9 %reduce-scatter.10.cloned.1.call-done = f32[128,768]{1,0:T(8,128)} async-done(((f32[1024,768]{1,0:T(8,128)}), f32[128,768]{1,0:T(8,128)}) %reduce-scatter.10.cloned.1.call-update) | async-done | bytes 393232 | tf_op jit(solution)/shard_map/reduce_scatter | solution.py:54
  487.0 3.2 fusion.8
  490.3 92.9 %reduce-scatter.12.cloned.1.call-done = f32[64,256]{1,0:T(8,128)} async-done(((f32[2048,256]{1,0:T(8,128)}), f32[64,256]{1,0:T(8,128)}) %reduce-scatter.12.cloned.1.call-update) | async-done | bytes 65552 | tf_op jit(solution)/shard_map/reduce_scatter | solution.py:87
  583.2 57.3 %all-gather.6.cloned.1.call-done = f32[2048,256]{1,0:T(8,128)} async-done(((f32[64,256]{1,0:T(8,128)}), f32[2048,256]{1,0:T(8,128)}) %all-gather.6.cloned.1.call-update) | async-done | bytes 2097168 | tf_op jit(solution)/shard_map/all_gather | solution.py:90
  640.5 3.1 copy.35
  643.6 4.3 all-to-all-start
  648.0 26.2 %all-to-all-done = f32[8,2,128,256]{3,2,1,0:T(8,128)} async-done(((f32[8,2,128,256]{3,2,1,0:T(8,128)}), f32[8,2,128,256]{3,2,1,0:T(8,128)}, u32[]{:S(2)}, u32[]{:S(2)}) %all-to-all-start) | async-done | bytes 2097184 | tf_op jit(solution)/shard_map/all_to_all | solution.py:93
  674.2 2.8 copy.16
  677.1 6.8 fusion.3
  685.4 65.5 %reduce-scatter.14.cloned.1.call-done = f32[256,704]{0,1:T(8,128)} async-done(((f32[2048,704]{0,1:T(8,128)}), f32[256,704]{0,1:T(8,128)}) %reduce-scatter.14.cloned.1.call-update) | async-done | bytes 720912 | tf_op jit(solution)/shard_map/reduce_scatter | solution.py:96
  (42 shorter events, 10.0 us)
Async XLA Ops:
  6.5 62.3 %all-gather.8.cloned.1.call-start = ((), (), s32[]{:S(2)}) async-start(), calls=%async_computation.14 | async-start | bytes 2162688 | tf_op jit(solution)/shard_map/all_gather | solution.py:39
  8.0 110.9 %reduce-scatter.6.cloned.1.call-start = ((), (), s32[]{:S(2)}) async-start(), calls=%async_computation.8 | async-start | bytes 3538944 | tf_op jit(solution)/shard_map/reduce_scatter | solution.py:47
  77.3 144.2 %all-gather.10.cloned.1.call-start = ((), (), s32[]{:S(2)}) async-start(), calls=%async_computation.15 | async-start | bytes 4718592 | tf_op jit(solution)/shard_map/all_gather | solution.py:43
  78.0 224.0 %all-reduce.3.cloned.1.call-start = ((), (), s32[]{:S(2)}) async-start(), calls=%async_computation.6 | async-start | bytes 1048576 | tf_op jit(solution)/shard_map/psum | solution.py:11
  83.2 271.2 %reduce-scatter.8.cloned.1.call-start = ((), (), s32[]{:S(2)}) async-start(), calls=%async_computation.9 | async-start | bytes 3538944 | tf_op jit(solution)/shard_map/reduce_scatter | solution.py:50
  124.3 310.0 %all-reduce.5.cloned.1.call-start = ((), (), s32[]{:S(2)}) async-start(), calls=%async_computation.7 | async-start | bytes 524288 | tf_op jit(solution)/shard_map/psum | solution.py:79
  124.3 230.0 %copy-start = (f32[1024,1,128]{2,1,0:T(1,128)S(1)}, f32[1024,1,128]{2,1,0:T(1,128)}, u32[]{:S(2)}) copy-start(f32[1024,1,128]{2,1,0:T(1,128)} %get-tuple-element.6) | copy-start | bytes 1572868
  304.3 181.9 %reduce-scatter.10.cloned.1.call-start = ((), (), s32[]{:S(2)}) async-start(), calls=%async_computation.10 | async-start | bytes 3538944 | tf_op jit(solution)/shard_map/reduce_scatter | solution.py:54
  354.4 79.9 %copy-start.3 = (f32[2048,64]{0,1:T(8,128)S(1)}, f32[2048,64]{0,1:T(8,128)}, u32[]{:S(2)}) copy-start(f32[2048,64]{0,1:T(8,128)} %all-reduce.3.cloned.1.call-done) | copy-start | bytes 1572868
  359.7 126.5 %copy-start.1 = (f32[128,768]{1,0:T(8,128)S(1)}, f32[128,768]{1,0:T(8,128)}, u32[]{:S(2)}) copy-start(f32[128,768]{1,0:T(8,128)} %reduce-scatter.6.cloned.1.call-done) | copy-start | bytes 1179652
  359.8 223.5 %reduce-scatter.12.cloned.1.call-start = ((), (), s32[]{:S(2)}) async-start(), calls=%async_computation.11 | async-start | bytes 2162688 | tf_op jit(solution)/shard_map/reduce_scatter | solution.py:87
  490.2 150.3 %all-gather.6.cloned.1.call-start = ((), (), s32[]{:S(2)}) async-start(), calls=%async_computation.12 | async-start | bytes 2162688 | tf_op jit(solution)/shard_map/all_gather | solution.py:90
  643.6 30.6 %all-to-all-start = ((f32[8,2,128,256]{3,2,1,0:T(8,128)}), f32[8,2,128,256]{3,2,1,0:T(8,128)}, u32[]{:S(2)}, u32[]{:S(2)}) async-start(f32[8,2,128,256]{3,2,1,0:T(8,128)} %bitcast.59), calls=%async_computation.4 | async-start | bytes 4194304 | tf_op jit(solution)/shard_map/all_to_all | solution.py:93
  648.0 29.1 %slice-start = ((f32[12,64,2,128]{3,2,1,0:T(2,128)}), f32[11,64,2,128]{3,2,1,0:T(2,128)S(1)}, s32[]{:S(2)}) async-start(f32[12,64,2,128]{3,2,1,0:T(2,128)} %param.3), calls=%async_computation.16 | async-start | bytes 1441792 | tf_op jit(solution)/shard_map/slice | solution.py:91
  648.0 102.9 %reduce-scatter.14.cloned.1.call-start = ((), (), s32[]{:S(2)}) async-start(), calls=%async_computation.13 | async-start | bytes 6488064 | tf_op jit(solution)/shard_map/reduce_scatter | solution.py:96
  683.8 1.0 copy-start.2
  684.8 67.2 %copy-start.4 = (f32[64,256]{1,0:T(8,128)S(1)}, f32[64,256]{1,0:T(8,128)}, u32[]{:S(2)}) copy-start(f32[64,256]{1,0:T(8,128)} %reduce-scatter.12.cloned.1.call-done) | copy-start | bytes 196612
Sparse Core Ops, SparseCore 0:
  9.9 58.8 all-gather.7
  77.4 41.4 reduce-scatter.5
  120.6 100.7 all-gather.9
  224.0 78.0 all-reduce.2
  304.7 49.6 reduce-scatter.7
  357.0 77.2 all-reduce.4
  436.8 49.2 reduce-scatter.9
  490.4 92.8 reduce-scatter.11
  585.8 54.6 all-gather.5
  684.0 66.8 reduce-scatter.13
where the time goes:
time: 761 us; the launch traced here: 760 us
  waiting for transfers between devices  685 us (90%)
  matrix products  32.9 us (4%)
  local copies, waits for them, and re-layouts  19.4 us (3%)
  between operations  13.7 us (2%)
    all_gather x1, waiting for transfers between devices, local(): inverse_all = lax.all_gather(second_cols, 'row', axis=1, tiled=True)  97.1 us
    reduce_scatter x1, waiting for transfers between devices, local(): lax.psum_scatter(times_rows(coeff_whole, lead_rows), 'col', scatter_dimen...  92.9 us
    psum x1, waiting for transfers between devices, spread(): return lax.psum(jnp.where(mine, array, jnp.zeros_like(array)), axis)  74.9 us
    psum x1, waiting for transfers between devices, local(): chained = lax.psum(partial_mix, 'row')  74.5 us
    reduce_scatter x1, waiting for transfers between devices, local(): lax.psum_scatter(times_rows_turned(turned_block, left_rows), 'row', scatt...  65.5 us
    all_gather x1, waiting for transfers between devices, local(): gathered = lax.all_gather(lower[0], 'col', axis=0, tiled=True)  59.5 us
    all_gather x1, waiting for transfers between devices, local(): everything = lax.all_gather(solved_lead, 'col', axis=0, tiled=True)  57.3 us
    reduce_scatter x1, waiting for transfers between devices, local(): lax.psum_scatter(times_rows(second_cols, remainder), 'row', scatter_dimen...  50.9 us
  transfers between devices with their start and end apart: 11, of which 11 were waited for; matrix products, arithmetic and copies ran while one was open for 3% of the time, Pallas kernels for 0%

commit v1 on v0

--- a/solution.py
+++ b/solution.py
@@ -76,7 +76,7 @@
     partial_mix = jnp.dot(
         mixed_cols, first_rows, precision=highest, preferred_element_type=jnp.float32
     )
-    chained = lax.psum(partial_mix, "row")
+    chained = jnp.sum(lax.all_gather(partial_mix, "row"), axis=0)
     coeff_whole = jnp.concatenate(
         [
             first_flag * mirrored[:block_size],

time: 761 us -> 725 us (0.953)
  waiting for transfers between devices: 685 us -> 647 us
    psum x1 -> x0, waiting for transfers between devices: 74.5 us -> none  [local(): chained = lax.psum(partial_mix, 'row')]
    all_gather x0 -> x1, waiting for transfers between devices: none -> 38.7 us  [local(): chained = jnp.sum(lax.all_gather(partial_mix, 'row'), axis=0)]
  transfers between devices with their start and end apart: 11 -> 11, of which waited for: 11 -> 11; matrix products, arithmetic and copies ran while one was open for 3% -> 4% of each run, Pallas kernels for 0% -> 0%
where the time goes in v1:
time: 725 us
  waiting for transfers between devices  647 us (89%)
  matrix products  32.8 us (5%)
  local copies, waits for them, and re-layouts  22.7 us (3%)
  between operations  13.8 us (2%)
    all_gather x1, waiting for transfers between devices, local(): inverse_all = lax.all_gather(second_cols, 'row', axis=1, tiled=True)  97.1 us
    reduce_scatter x1, waiting for transfers between devices, local(): lax.psum_scatter(times_rows(coeff_whole, lead_rows), 'col', scatter_dimen...  93.2 us
    psum x1, waiting for transfers between devices, spread(): return lax.psum(jnp.where(mine, array, jnp.zeros_like(array)), axis)  74.9 us
    reduce_scatter x1, waiting for transfers between devices, local(): lax.psum_scatter(times_rows_turned(turned_block, left_rows), 'row', scatt...  65.5 us
    all_gather x1, waiting for transfers between devices, local(): gathered = lax.all_gather(lower[0], 'col', axis=0, tiled=True)  59.5 us
    all_gather x1, waiting for transfers between devices, local(): everything = lax.all_gather(solved_lead, 'col', axis=0, tiled=True)  57.5 us
    reduce_scatter x1, waiting for transfers between devices, local(): lax.psum_scatter(times_rows(cross_cols, upper_half), 'row', scatter_dimen...  49.9 us
    reduce_scatter x1, waiting for transfers between devices, local(): lax.psum_scatter(times_rows(second_cols, remainder), 'row', scatter_dimen...  47.8 us
  transfers between devices with their start and end apart: 11, of which 11 were waited for; matrix products, arithmetic and copies ran while one was open for 4% of the time, Pallas kernels for 0%

profile of v1, /device:TPU:1, one launch (start us, length us, event | category | flops | bytes accessed | tf_op | source)
XLA Modules:
  0.0 724.8 jit_solution(7264689366832184464)
XLA Ops:
  9.3 59.5 %all-gather.10.cloned.1.call-done = f32[1,2048,2,128]{3,2,0,1:T(2,128)} async-done(((f32[1,64,2,128]{3,2,0,1:T(2,128)}), f32[1,2048,2,128]{3,2,0,1:T(2,128)}) %all-gather.10.cloned.1.call-update) | async-done | bytes 2097168 | tf_op jit(solution)/shard_map/all_gather | solution.py:39
  68.8 4.1 fusion.20
  73.0 4.3 fusion.14
  78.2 3.5 constant_dynamic-slice_fusion
  83.2 35.7 %reduce-scatter.6.cloned.1.call-done = f32[128,768]{1,0:T(8,128)} async-done(((f32[1024,768]{1,0:T(8,128)}), f32[128,768]{1,0:T(8,128)}) %reduce-scatter.6.cloned.1.call-update) | async-done | bytes 393232 | tf_op jit(solution)/shard_map/reduce_scatter | solution.py:47
  118.9 5.3 convolution_bitcast_fusion.1
  124.3 97.1 %all-gather.12.cloned.1.call-done = f32[1024,1,1024]{2,1,0:T(1,128)} async-done(((f32[1024,1,128]{2,1,0:T(1,128)}), f32[1024,1,1024]{2,1,0:T(1,128)}) %all-gather.12.cloned.1.call-update) | async-done | bytes 4194320 | tf_op jit(solution)/shard_map/all_gather | solution.py:43
  221.5 5.7 fusion
  227.2 74.9 %all-reduce.2.cloned.1.call-done = f32[2048,64]{0,1:T(8,128)} async-done(((f32[2048,64]{0,1:T(8,128)}), f32[2048,64]{0,1:T(8,128)}) %all-reduce.2.cloned.1.call-update) | async-done | bytes 524304 | tf_op jit(solution)/shard_map/psum | solution.py:11
  302.1 2.2 fusion.16
  304.5 49.9 %reduce-scatter.8.cloned.1.call-done = f32[128,768]{0,1:T(8,128)} async-done(((f32[1024,768]{0,1:T(8,128)}), f32[128,768]{0,1:T(8,128)}) %reduce-scatter.8.cloned.1.call-update) | async-done | bytes 393232 | tf_op jit(solution)/shard_map/reduce_scatter | solution.py:50
  354.4 5.3 convolution_bitcast_fusion
  359.7 38.7 %all-gather.14.cloned.1.call-done = f32[8192,64]{0,1:T(8,128)} async-done(((f32[1024,64]{0,1:T(8,128)}), f32[8192,64]{0,1:T(8,128)}) %all-gather.14.cloned.1.call-update) | async-done | bytes 2097168 | tf_op jit(solution)/shard_map/all_gather | solution.py:79
  398.4 2.8 copy.20
  402.3 47.8 %reduce-scatter.10.cloned.1.call-done = f32[128,768]{1,0:T(8,128)} async-done(((f32[1024,768]{1,0:T(8,128)}), f32[128,768]{1,0:T(8,128)}) %reduce-scatter.10.cloned.1.call-update) | async-done | bytes 393232 | tf_op jit(solution)/shard_map/reduce_scatter | solution.py:54
  451.0 3.2 fusion.8
  454.2 93.2 %reduce-scatter.12.cloned.1.call-done = f32[64,256]{1,0:T(8,128)} async-done(((f32[2048,256]{1,0:T(8,128)}), f32[64,256]{1,0:T(8,128)}) %reduce-scatter.12.cloned.1.call-update) | async-done | bytes 65552 | tf_op jit(solution)/shard_map/reduce_scatter | solution.py:87
  547.5 57.5 %all-gather.8.cloned.1.call-done = f32[2048,256]{1,0:T(8,128)} async-done(((f32[64,256]{1,0:T(8,128)}), f32[2048,256]{1,0:T(8,128)}) %all-gather.8.cloned.1.call-update) | async-done | bytes 2097168 | tf_op jit(solution)/shard_map/all_gather | solution.py:90
  605.0 3.1 copy.36
  608.1 4.3 all-to-all-start
  612.5 26.2 %all-to-all-done = f32[8,2,128,256]{3,2,1,0:T(8,128)} async-done(((f32[8,2,128,256]{3,2,1,0:T(8,128)}), f32[8,2,128,256]{3,2,1,0:T(8,128)}, u32[]{:S(2)}, u32[]{:S(2)}) %all-to-all-start) | async-done | bytes 2097184 | tf_op jit(solution)/shard_map/all_to_all | solution.py:93
  638.7 2.8 copy.16
  641.6 6.8 fusion.3
  649.9 65.5 %reduce-scatter.14.cloned.1.call-done = f32[256,704]{0,1:T(8,128)} async-done(((f32[2048,704]{0,1:T(8,128)}), f32[256,704]{0,1:T(8,128)}) %reduce-scatter.14.cloned.1.call-update) | async-done | bytes 720912 | tf_op jit(solution)/shard_map/reduce_scatter | solution.py:96
  (44 shorter events, 11.5 us)
Async XLA Ops:
  6.5 62.3 %all-gather.10.cloned.1.call-start = ((), (), s32[]{:S(2)}) async-start(), calls=%async_computation.13 | async-start | bytes 2162688 | tf_op jit(solution)/shard_map/all_gather | solution.py:39
  8.0 110.9 %reduce-scatter.6.cloned.1.call-start = ((), (), s32[]{:S(2)}) async-start(), calls=%async_computation.7 | async-start | bytes 3538944 | tf_op jit(solution)/shard_map/reduce_scatter | solution.py:47
  77.3 144.2 %all-gather.12.cloned.1.call-start = ((), (), s32[]{:S(2)}) async-start(), calls=%async_computation.14 | async-start | bytes 4718592 | tf_op jit(solution)/shard_map/all_gather | solution.py:43
  78.0 224.0 %all-reduce.2.cloned.1.call-start = ((), (), s32[]{:S(2)}) async-start(), calls=%async_computation.6 | async-start | bytes 1048576 | tf_op jit(solution)/shard_map/psum | solution.py:11
  83.2 271.2 %reduce-scatter.8.cloned.1.call-start = ((), (), s32[]{:S(2)}) async-start(), calls=%async_computation.8 | async-start | bytes 3538944 | tf_op jit(solution)/shard_map/reduce_scatter | solution.py:50
  124.3 274.2 %all-gather.14.cloned.1.call-start = ((), (), s32[]{:S(2)}) async-start(), calls=%async_computation.15 | async-start | bytes 2359296 | tf_op jit(solution)/shard_map/all_gather | solution.py:79
  124.3 230.0 %copy-start = (f32[1024,1,128]{2,1,0:T(1,128)S(1)}, f32[1024,1,128]{2,1,0:T(1,128)}, u32[]{:S(2)}) copy-start(f32[1024,1,128]{2,1,0:T(1,128)} %get-tuple-element.6) | copy-start | bytes 1572868
  304.3 145.8 %reduce-scatter.10.cloned.1.call-start = ((), (), s32[]{:S(2)}) async-start(), calls=%async_computation.9 | async-start | bytes 3538944 | tf_op jit(solution)/shard_map/reduce_scatter | solution.py:54
  359.7 187.7 %reduce-scatter.12.cloned.1.call-start = ((), (), s32[]{:S(2)}) async-start(), calls=%async_computation.10 | async-start | bytes 2162688 | tf_op jit(solution)/shard_map/reduce_scatter | solution.py:87
  401.2 1.0 copy-start.3
  401.2 48.9 %copy-start.1 = (f32[128,768]{1,0:T(8,128)S(1)}, f32[128,768]{1,0:T(8,128)}, u32[]{:S(2)}) copy-start(f32[128,768]{1,0:T(8,128)} %reduce-scatter.6.cloned.1.call-done) | copy-start | bytes 1179652
  454.2 150.8 %all-gather.8.cloned.1.call-start = ((), (), s32[]{:S(2)}) async-start(), calls=%async_computation.11 | async-start | bytes 2162688 | tf_op jit(solution)/shard_map/all_gather | solution.py:90
  608.1 30.6 %all-to-all-start = ((f32[8,2,128,256]{3,2,1,0:T(8,128)}), f32[8,2,128,256]{3,2,1,0:T(8,128)}, u32[]{:S(2)}, u32[]{:S(2)}) async-start(f32[8,2,128,256]{3,2,1,0:T(8,128)} %bitcast.64), calls=%async_computation.4 | async-start | bytes 4194304 | tf_op jit(solution)/shard_map/all_to_all | solution.py:93
  612.5 102.9 %reduce-scatter.14.cloned.1.call-start = ((), (), s32[]{:S(2)}) async-start(), calls=%async_computation.12 | async-start | bytes 6488064 | tf_op jit(solution)/shard_map/reduce_scatter | solution.py:96
  612.5 29.0 %slice-start = ((f32[12,64,2,128]{3,2,1,0:T(2,128)}), f32[11,64,2,128]{3,2,1,0:T(2,128)S(1)}, s32[]{:S(2)}) async-start(f32[12,64,2,128]{3,2,1,0:T(2,128)} %param.3), calls=%async_computation.16 | async-start | bytes 1441792 | tf_op jit(solution)/shard_map/slice | solution.py:91
  648.3 1.0 copy-start.2
  649.6 67.0 %copy-start.4 = (f32[64,256]{1,0:T(8,128)S(1)}, f32[64,256]{1,0:T(8,128)}, u32[]{:S(2)}) copy-start(f32[64,256]{1,0:T(8,128)} %reduce-scatter.12.cloned.1.call-done) | copy-start | bytes 196612
Sparse Core Ops, SparseCore 0:
  9.9 58.8 all-gather.9
  77.4 41.4 reduce-scatter.5
  120.6 100.7 all-gather.11
  224.0 78.0 all-reduce.1
  304.7 49.6 reduce-scatter.7
  356.2 42.2 all-gather.13
  401.2 48.8 reduce-scatter.9
  454.4 92.9 reduce-scatter.11
  550.3 54.6 all-gather.7
  648.5 66.8 reduce-scatter.13
